TPU v7x, 512 devices: a whole 4x8x8 slice. The times are simulated.
512 devices in a mesh: col: 64 (over z_lo, y, core), row: 8 (over x, z_hi).
Axes of the slice: x: 4, y: 8, z: 8 (z_hi: 2, z_lo: 4; z = z_hi * 4 + z_lo), core: 2. Of those that a mesh axis runs over, the one named last changes fastest.
Arguments:
- image: bfloat16 [96, 64, 8192], P(None, 'row', 'col'), may hold values from -6 to 6
- cotangent: bfloat16 [96, 64, 8192], P(None, 'row', 'col'), may hold values from -6 to 6
- dw_kernel: float32 [96, 7, 7], replicated, may hold values from -0.875 to 0.875
- dw_bias: float32 [96], replicated, may hold values from -3 to 3
- ln_gain: float32 [96], replicated, may hold values from 0.1 to 1.9
- ln_bias: float32 [96], replicated, may hold values from -3 to 3
- w_in: bfloat16 [96, 384], replicated, may hold values from -0.625 to 0.625
- b_in: float32 [384], replicated, may hold values from -3 to 3
- w_out: bfloat16 [384, 96], replicated, may hold values from -0.3125 to 0.3125
- layer_scale: float32 [96], replicated, may hold values from 0.5 to 2
Outputs:
- block_out: bfloat16 [96, 64, 8192], P(None, 'row', 'col')
- image_grad: bfloat16 [96, 64, 8192], P(None, 'row', 'col')
- kernel_grad: float32 [96, 7, 7], replicated
- dw_bias_grad: float32 [96], replicated
- gain_grad: float32 [96], replicated
- ln_bias_grad: float32 [96], replicated
- w_in_grad: float32 [96, 384], replicated
- b_in_grad: float32 [384], replicated
- w_out_grad: float32 [384, 96], replicated
- scale_grad: float32 [96], replicated
All inputs are finite; a program needn't handle non-finite values.
Results may differ from a plain program's by a relative error of at most 0.0065.
Values may be sent and summed in bfloat16 or wider, within the bound.
No kernel may reach another device: no remote copies, remote signals or barrier semaphores. Data moves between devices by JAX's collectives and lax.ppermute only.
A program may use at most 64 MiB of HBM per device.

v0:
```python
import math
import jax
import jax.numpy as jnp
from jax import lax
from jax.sharding import PartitionSpec as P


def padded_2(block, sides, width):
    for axis, dim in sides:
        count = lax.axis_size(axis)
        forward = [(i, i + 1) for i in range(count - 1)]
        backward = [(target, source) for source, target in forward]
        low = lax.ppermute(
            lax.slice_in_dim(block, block.shape[dim] - width, None, axis=dim), axis, forward
        )
        high = lax.ppermute(lax.slice_in_dim(block, 0, width, axis=dim), axis, backward)
        block = jnp.concatenate([low, block, high], axis=dim)
    return block


def from_behind(value, axis, steps):
    count = lax.axis_size(axis)
    initial, last = (max(0, -steps), min(count, count - steps))
    return lax.ppermute(value, axis, [(source, source + steps) for source in range(initial, last)])


def conv_seven(padded, kernel):
    height = padded.shape[1] - 6
    breadth = padded.shape[2] - 6
    summed = jnp.zeros((padded.shape[0], height, breadth), jnp.float32)
    for row_step in range(7):
        for col_step in range(7):
            summed = (
                summed
                + kernel[:, row_step, col_step][:, None, None]
                * padded[:, row_step : row_step + height, col_step : col_step + breadth]
            )
    return summed


def kernel_terms(conv_grad, padded):
    height, breadth = (conv_grad.shape[1], conv_grad.shape[2])
    pieces = []
    for row_step in range(7):
        for col_step in range(7):
            pieces.append(
                jnp.sum(
                    conv_grad
                    * padded[:, row_step : row_step + height, col_step : col_step + breadth],
                    axis=(1, 2),
                )
            )
    return jnp.stack(pieces, axis=1).reshape(conv_grad.shape[0], 7, 7)


def product(form, left, right):
    return jnp.einsum(form, left, right, preferred_element_type=jnp.float32)


def mixing(conv_flat, image_flat, cotan_flat, ln_gain, ln_bias, w_in, b_in, w_out, layer_scale):
    average = jnp.mean(conv_flat, axis=0, keepdims=True)
    centred = conv_flat - average
    spread = jnp.mean(centred * centred, axis=0, keepdims=True)
    inverse = lax.rsqrt(spread + 1e-06)
    normed = centred * inverse
    ln_out = (normed * ln_gain[:, None] + ln_bias[:, None]).astype(jnp.bfloat16)
    pre_act = product("ch,cp->hp", w_in, ln_out) + b_in[:, None]
    act_out, gelu_pull = jax.vjp(jax.nn.gelu, pre_act)
    activ = act_out.astype(jnp.bfloat16)
    branch = product("hc,hp->cp", w_out, activ)
    scale_col = layer_scale[:, None]
    block_out = (image_flat.astype(jnp.float32) + scale_col * branch).astype(jnp.bfloat16)
    upstream = cotan_flat.astype(jnp.float32)
    scale_sum = jnp.sum(upstream * branch, axis=1)
    branch_grad = (scale_col * upstream).astype(jnp.bfloat16)
    w_out_sum = product("hp,cp->hc", activ, branch_grad)
    act_grad = product("hc,cp->hp", w_out, branch_grad)
    pre_grad = gelu_pull(act_grad)[0].astype(jnp.bfloat16)
    b_in_sum = jnp.sum(pre_grad.astype(jnp.float32), axis=1)
    w_in_sum = product("cp,hp->ch", ln_out, pre_grad)
    ln_grad = product("ch,hp->cp", w_in, pre_grad)
    gain_sum = jnp.sum(ln_grad * normed, axis=1)
    shift_sum = jnp.sum(ln_grad, axis=1)
    normed_grad = ln_grad * ln_gain[:, None]
    conv_grad = inverse * (
        normed_grad
        - jnp.mean(normed_grad, axis=0, keepdims=True)
        - normed * jnp.mean(normed_grad * normed, axis=0, keepdims=True)
    )
    return (block_out, conv_grad, (gain_sum, shift_sum, w_in_sum, b_in_sum, w_out_sum, scale_sum))


def local(image, cotangent, dw_kernel, dw_bias, ln_gain, ln_bias, w_in, b_in, w_out, layer_scale):
    channels, height, breadth = image.shape
    pixels = height * breadth
    padded = padded_2(image, (("col", 2), ("row", 1)), 3)
    conv_out = conv_seven(padded, dw_kernel) + dw_bias[:, None, None]
    block_flat, grad_flat, sums = mixing(
        conv_out.reshape(channels, pixels),
        image.reshape(channels, pixels),
        cotangent.reshape(channels, pixels),
        ln_gain,
        ln_bias,
        w_in,
        b_in,
        w_out,
        layer_scale,
    )
    gain_sum, shift_sum, w_in_sum, b_in_sum, w_out_sum, scale_sum = sums
    block_out = block_flat.reshape(channels, height, breadth)
    conv_grad = grad_flat.reshape(channels, height, breadth)
    flipped = dw_kernel[:, ::-1, ::-1]
    extended = conv_seven(jnp.pad(conv_grad, ((0, 0), (6, 6), (6, 6))), flipped)
    from_above = from_behind(extended[:, height + 3 :, :].astype(jnp.bfloat16), "row", 1).astype(
        jnp.float32
    )
    from_below = from_behind(extended[:, :3, :].astype(jnp.bfloat16), "row", -1).astype(jnp.float32)
    middle = extended[:, 3 : height + 3, :]
    middle = middle.at[:, :3, :].add(from_above)
    middle = middle.at[:, height - 3 :, :].add(from_below)
    from_left = from_behind(middle[:, :, breadth + 3 :], "col", 1)
    from_right = from_behind(middle[:, :, :3], "col", -1)
    back = middle[:, :, 3 : breadth + 3]
    back = back.at[:, :, :3].add(from_left)
    back = back.at[:, :, breadth - 3 :].add(from_right)
    image_grad = (cotangent.astype(jnp.float32) + back).astype(jnp.bfloat16)
    kernel_sum = kernel_terms(conv_grad, padded)
    bias_sum = jnp.sum(conv_grad, axis=(1, 2))
    kernel_sum, bias_sum, gain_sum, shift_sum, w_in_sum, b_in_sum, w_out_sum, scale_sum = lax.psum(
        (kernel_sum, bias_sum, gain_sum, shift_sum, w_in_sum, b_in_sum, w_out_sum, scale_sum),
        ("col", "row"),
    )
    factor = 1.0 / math.sqrt(height * lax.axis_size("row") * breadth * lax.axis_size("col"))
    return (
        block_out,
        image_grad,
        factor * kernel_sum,
        factor * bias_sum,
        factor * gain_sum,
        factor * shift_sum,
        factor * w_in_sum,
        factor * b_in_sum,
        factor * w_out_sum,
        factor * scale_sum,
    )


def solution(mesh):
    in_specs = (
        P(None, "row", "col"),
        P(None, "row", "col"),
        P(),
        P(),
        P(),
        P(),
        P(),
        P(),
        P(),
        P(),
    )
    out_specs = (
        P(None, "row", "col"),
        P(None, "row", "col"),
        P(),
        P(),
        P(),
        P(),
        P(),
        P(),
        P(),
        P(),
    )
    return jax.shard_map(local, mesh=mesh, in_specs=in_specs, out_specs=out_specs, check_vma=False)
```

profile of v0, /device:TPU:1, one launch (start us, length us, event | category | flops | bytes accessed | tf_op | source)
XLA Modules:
  0.0 492.2 jit_solution(10161626249035542997)
XLA Ops:
  7.2 1.1 copy.20
  8.4 4.6 collective-permute-start
  13.0 5.5 %collective-permute-start.1 = (bf16[96,8,3]{0,2,1:T(4,128)(2,1)S(1)}, bf16[96,8,3]{0,2,1:T(4,128)(2,1)S(1)}, u32[]{:S(2)}, u32[]{:S(2)}) collective-permute-start(bf16[96,8,3]{0,2,1:T(4,128)(2,1)S(1)} %get-tuple-element.145), channel_id=1, source_target_pairs={{8,0},{16,8},{24,16},{32,24},{40,32},{48,40},{56,48},{64,56},{72,6... | collective-permute-start | bytes 13832 | tf_op jit(solution)/shard_map/ppermute | solution.py:16
  18.5 1.0 slice_bitcast_fusion.48
  19.5 1.0 slice_bitcast_fusion.47
  20.6 8.1 %collective-permute-start.2 = (bf16[96,3,134]{0,2,1:T(8,128)(2,1)S(1)}, bf16[96,3,134]{0,2,1:T(8,128)(2,1)S(1)}, u32[]{:S(2)}, u32[]{:S(2)}) collective-permute-start(bf16[96,3,134]{0,2,1:T(8,128)(2,1)S(1)} %get-tuple-element.142), channel_id=1, source_target_pairs={{0,1},{1,2},{2,3},{3,4},{4,5},{5,6},{6,7},{8,9},{9,10},{10,11},{11... | collective-permute-start | bytes 231560 | tf_op jit(solution)/shard_map/ppermute | solution.py:13
  28.7 1.3 collective-permute-start.3
  30.0 0.9 slice_bitcast_fusion.46
  30.9 1.0 convert.8
  31.9 0.9 copy.77
  32.8 7.5 %collective-permute-done.3 = bf16[96,3,134]{0,2,1:T(8,128)(2,1)S(1)} collective-permute-done((bf16[96,3,134]{0,2,1:T(8,128)(2,1)S(1)}, bf16[96,3,134]{0,2,1:T(8,128)(2,1)S(1)}, u32[]{:S(2)}, u32[]{:S(2)}) %collective-permute-start.3) | collective-permute-done | bytes 77216 | tf_op jit(solution)/shard_map/ppermute | solution.py:16
  40.5 4.3 fusion.223
  44.8 0.4 multiply_reduce_fusion.1
  45.4 1.7 fusion.107
  47.1 2.0 convert_reduce_fusion
  49.1 1.0 fusion.220
  50.1 0.4 fusion.208
  50.5 0.3 fusion.207
  51.1 1.9 fusion.203
  53.0 1.9 fusion.153
  54.8 0.8 fusion.135
  55.8 23.9 %fusion.221 = (bf16[96,14,134]{2,1,0:T(8,128)(2,1)}, f32[96,14,134]{2,1,0:T(8,128)S(1)}) fusion(f32[96]{0:T(128)S(1)} %get-tuple-element.146, f32[96]{0:T(128)S(1)} %get-tuple-element.165, f32[96]{0:T(128)S(1)} %get-tuple-element.184, f32[96]{0:T(128)S(1)} %get-tuple-element.192, f32[96]{0:T(128)S(1)} %get-tuple-element.191, f32[96]{0:T(128)S(1)} %get-tuple-element.190, ...), kind=kLoop, calls=%fused_computation.460 | loop fusion | flops 17649408 | bytes 1492608 | tf_op jit(solution)/shard_map/convert.3
  80.1 1.0 fusion.215
  81.1 1.0 fusion.185
  82.6 1.9 fusion.206
  84.5 100.3 %all-reduce.1 = (f32[96,7,7]{0,2,1:T(8,128)S(1)}, f32[96]{0:T(128)S(1)}, f32[96]{0:T(128)S(1)}, f32[96]{0:T(128)S(1)}, f32[384]{0:T(512)S(1)}, /*index=5*/f32[96]{0:T(128)S(1)}) all-reduce(f32[96,7,7]{0,2,1:T(8,128)S(1)} %reshape.203, f32[96]{0:T(128)S(1)} %get-tuple-element.101, ...), channel_id=1, replica_groups=mesh['col'=64,'row'=8] {'col','row'}, use_global_device_ids=true, to_apply=%region_53.54 | all-reduce | flops 5472 | bytes 43776 | tf_op jit(solution)/shard_map/psum | solution.py:129
  184.8 0.6 broadcast_multiply_fusion.2
  185.4 0.6 broadcast_multiply_fusion.6
  186.0 0.5 broadcast_multiply_fusion.10
  186.5 0.5 broadcast_multiply_fusion.7
  187.2 3.4 collective-permute-start.4
  190.6 0.5 broadcast_multiply_fusion.8
  191.3 1.3 collective-permute-start.5
  192.6 3.4 collective-permute-done.4
  196.1 2.6 scatter-add.14
  198.7 8.0 %collective-permute-done.5 = bf16[96,3,134]{2,1,0:T(4,128)(2,1)S(1)} collective-permute-done((bf16[96,3,134]{2,1,0:T(4,128)(2,1)S(1)}, bf16[96,3,134]{2,1,0:T(4,128)(2,1)S(1)}, u32[]{:S(2)}, u32[]{:S(2)}) %collective-permute-start.5) | collective-permute-done | bytes 77216 | tf_op jit(solution)/shard_map/ppermute | solution.py:24
  206.8 2.6 scatter-add.15
  209.5 4.8 collective-permute-start.6
  214.3 0.5 broadcast_multiply_fusion.9
  214.8 0.7 copy.79
  215.7 1.9 collective-permute-start.7
  217.6 1.4 collective-permute-done.6
  219.2 6.1 %scatter-add.16 = f32[96,8,128]{2,1,0:T(8,128)S(1)} dynamic-update-slice(f32[96,8,128]{2,1,0:T(8,128)S(1)} %slice.979, f32[96,8,3]{2,1,0:T(8,128)S(1)} %slice_add_fusion.1, s32[]{:T(128)} %constant.134.clone.1, s32[]{:T(128)} %constant.134.clone.1, s32[]{:T(128)} %constant.134.clone.1) | dynamic-update-slice | bytes 18436 | tf_op jit(solution)/shard_map/scatter-add | solution.py:124
  225.4 18.6 %scatter-add.19 = f32[96,8,128]{2,1,0:T(8,128)S(1)} dynamic-update-slice(f32[96,8,128]{2,1,0:T(8,128)S(1)} %scatter-add.16, f32[96,8,3]{2,1,0:T(8,128)S(1)} %slice_add_fusion, s32[]{:T(128)} %constant.134.clone.1, s32[]{:T(128)} %constant.134.clone.1, s32[]{:T(128)} %constant.136.clone.1) | dynamic-update-slice | bytes 18436 | tf_op jit(solution)/shard_map/scatter-add | solution.py:125
  244.0 0.7 add_convert_fusion
  244.7 237.4 %all-reduce.5.cloned.1.call-done = (f32[96,384]{1,0:T(8,128)}, f32[384,96]{0,1:T(8,128)}) async-done(((f32[96,384]{1,0:T(8,128)}, f32[384,96]{0,1:T(8,128)}), (f32[96,384]{1,0:T(8,128)}, f32[384,96]{0,1:T(8,128)})) %all-reduce.5.cloned.1.call-update) | async-done | bytes 294928 | tf_op jit(solution)/shard_map/psum | solution.py:129
  482.2 1.6 broadcast_multiply_fusion
  483.8 1.6 broadcast_multiply_fusion.1
  (114 shorter events, 2.7 us)
Async XLA Ops:
  7.2 38.2 %copy-start = (bf16[96,384]{1,0:T(8,128)(2,1)S(1)}, bf16[96,384]{1,0:T(8,128)(2,1)}, u32[]{:S(2)}) copy-start(bf16[96,384]{1,0:T(8,128)(2,1)} %param.24) | copy-start | bytes 221188
  7.2 475.0 %all-reduce.5.cloned.1.call-start = ((), (), s32[]{:S(2)}) async-start(), calls=%async_computation | async-start | bytes 589824 | tf_op jit(solution)/shard_map/psum | solution.py:129
  8.4 32.1 %copy-start.41 = (f32[96]{0:T(128)S(1)}, f32[96]{0:T(128)}, u32[]{:S(2)}) copy-start(f32[96]{0:T(128)} %param.21) | copy-start | bytes 1156
  8.4 12.1 %collective-permute-start = (bf16[96,8,3]{0,2,1:T(4,128)(2,1)S(1)}, bf16[96,8,3]{0,2,1:T(4,128)(2,1)S(1)}, u32[]{:S(2)}, u32[]{:S(2)}) collective-permute-start(bf16[96,8,3]{0,2,1:T(4,128)(2,1)S(1)} %get-tuple-element.144), channel_id=1, source_target_pairs={{0,8},{8,16},{16,24},{24,32},{32,40},{40,48},{48,56},{56,64},{64,7... | collective-permute-start | bytes 13832 | tf_op jit(solution)/shard_map/ppermute | solution.py:13
  13.0 7.5 %collective-permute-start.1 = (bf16[96,8,3]{0,2,1:T(4,128)(2,1)S(1)}, bf16[96,8,3]{0,2,1:T(4,128)(2,1)S(1)}, u32[]{:S(2)}, u32[]{:S(2)}) collective-permute-start(bf16[96,8,3]{0,2,1:T(4,128)(2,1)S(1)} %get-tuple-element.145), channel_id=1, source_target_pairs={{8,0},{16,8},{24,16},{32,24},{40,32},{48,40},{56,48},{64,56},{72,6... | collective-permute-start | bytes 13832 | tf_op jit(solution)/shard_map/ppermute | solution.py:16
  20.6 12.2 %collective-permute-start.2 = (bf16[96,3,134]{0,2,1:T(8,128)(2,1)S(1)}, bf16[96,3,134]{0,2,1:T(8,128)(2,1)S(1)}, u32[]{:S(2)}, u32[]{:S(2)}) collective-permute-start(bf16[96,3,134]{0,2,1:T(8,128)(2,1)S(1)} %get-tuple-element.142), channel_id=1, source_target_pairs={{0,1},{1,2},{2,3},{3,4},{4,5},{5,6},{6,7},{8,9},{9,10},{10,11},{11... | collective-permute-start | bytes 231560 | tf_op jit(solution)/shard_map/ppermute | solution.py:13
  28.7 11.6 %collective-permute-start.3 = (bf16[96,3,134]{0,2,1:T(8,128)(2,1)S(1)}, bf16[96,3,134]{0,2,1:T(8,128)(2,1)S(1)}, u32[]{:S(2)}, u32[]{:S(2)}) collective-permute-start(bf16[96,3,134]{0,2,1:T(8,128)(2,1)S(1)} %get-tuple-element.143), channel_id=1, source_target_pairs={{1,0},{2,1},{3,2},{4,3},{5,4},{6,5},{7,6},{9,8},{10,9},{11,10},{12... | collective-permute-start | bytes 231560 | tf_op jit(solution)/shard_map/ppermute | solution.py:16
  31.9 15.3 %copy-start.3 = (f32[12,8,8,128]{3,2,1,0:T(8,128)}, f32[12,8,8,128]{3,2,1,0:T(8,128)S(1)}, u32[]{:S(2)}) copy-start(f32[12,8,8,128]{3,2,1,0:T(8,128)S(1)} %convert.8) | copy-start | bytes 1179652
  40.5 4.9 copy-start.9
  40.5 4.9 copy-start.42
  40.5 4.9 copy-start.43
  55.8 24.2 %copy-start.4 = (f32[12,8,8,128]{3,2,1,0:T(8,128)S(1)}, f32[12,8,8,128]{3,2,1,0:T(8,128)}, u32[]{:S(2)}) copy-start(f32[12,8,8,128]{3,2,1,0:T(8,128)} %copy-done.3) | copy-start | bytes 1179652
  55.8 24.2 %copy-start.5 = (bf16[384,1024]{0,1:T(8,128)(2,1)S(1)}, bf16[384,1024]{0,1:T(8,128)(2,1)}, u32[]{:S(2)}) copy-start(bf16[384,1024]{0,1:T(8,128)(2,1)} %get-tuple-element.197) | copy-start | bytes 2359300
  79.7 2.3 copy-start.12
  79.8 2.3 copy-start.13
  79.8 2.3 copy-start.14
  79.8 2.3 copy-start.15
  79.8 2.3 copy-start.16
  79.8 2.3 copy-start.17
  79.8 2.3 copy-start.18
  79.8 2.3 copy-start.19
  79.8 2.3 copy-start.20
  79.8 2.3 copy-start.21
  79.8 2.3 copy-start.22
  79.9 2.3 copy-start.23
  79.9 2.3 copy-start.24
  79.9 2.3 copy-start.25
  79.9 2.3 copy-start.26
  79.9 2.3 copy-start.27
  79.9 2.3 copy-start.28
  79.9 2.3 copy-start.29
  79.9 2.3 copy-start.30
  79.9 2.3 copy-start.31
  79.9 2.3 copy-start.32
  80.0 2.3 copy-start.33
  80.0 2.3 copy-start.34
  80.0 2.3 copy-start.35
  80.0 2.3 copy-start.36
  80.0 2.3 copy-start.37
  80.0 2.3 copy-start.38
  80.0 2.3 copy-start.39
  82.0 2.4 copy-start.40
  82.0 105.0 %copy-start.6 = (bf16[96,14,134]{2,1,0:T(8,128)(2,1)S(1)}, bf16[96,14,134]{2,1,0:T(8,128)(2,1)}, u32[]{:S(2)}) copy-start(bf16[96,14,134]{2,1,0:T(8,128)(2,1)} %get-tuple-element.129) | copy-start | bytes 1080580
  187.2 8.8 %collective-permute-start.4 = (bf16[96,3,134]{2,1,0:T(4,128)(2,1)S(1)}, bf16[96,3,134]{2,1,0:T(4,128)(2,1)S(1)}, u32[]{:S(2)}, u32[]{:S(2)}) collective-permute-start(bf16[96,3,134]{2,1,0:T(4,128)(2,1)S(1)} %get-tuple-element.137), channel_id=1, source_target_pairs={{0,1},{1,2},{2,3},{3,4},{4,5},{5,6},{6,7},{8,9},{9,10},{10,11},{11... | collective-permute-start | bytes 231560 | tf_op jit(solution)/shard_map/ppermute | solution.py:24
  191.3 15.4 %collective-permute-start.5 = (bf16[96,3,134]{2,1,0:T(4,128)(2,1)S(1)}, bf16[96,3,134]{2,1,0:T(4,128)(2,1)S(1)}, u32[]{:S(2)}, u32[]{:S(2)}) collective-permute-start(bf16[96,3,134]{2,1,0:T(4,128)(2,1)S(1)} %get-tuple-element.136), channel_id=1, source_target_pairs={{1,0},{2,1},{3,2},{4,3},{5,4},{6,5},{7,6},{9,8},{10,9},{11,10},{12... | collective-permute-start | bytes 231560 | tf_op jit(solution)/shard_map/ppermute | solution.py:24
  209.5 9.5 %collective-permute-start.6 = (f32[96,8,3]{2,1,0:T(8,128)S(1)}, f32[96,8,3]{2,1,0:T(8,128)S(1)}, u32[]{:S(2)}, u32[]{:S(2)}) collective-permute-start(f32[96,8,3]{2,1,0:T(8,128)S(1)} %get-tuple-element.135), channel_id=1, source_target_pairs={{0,8},{8,16},{16,24},{24,32},{32,40},{40,48},{48,56},{56,64},{64,7... | collective-permute-start | bytes 27656 | tf_op jit(solution)/shard_map/ppermute | solution.py:24
  215.7 9.6 %collective-permute-start.7 = (f32[96,8,3]{2,1,0:T(8,128)S(1)}, f32[96,8,3]{2,1,0:T(8,128)S(1)}, u32[]{:S(2)}, u32[]{:S(2)}) collective-permute-start(f32[96,8,3]{2,1,0:T(8,128)S(1)} %get-tuple-element.134), channel_id=1, source_target_pairs={{8,0},{16,8},{24,16},{32,24},{40,32},{48,40},{56,48},{64,56},{72,6... | collective-permute-start | bytes 27656 | tf_op jit(solution)/shard_map/ppermute | solution.py:24
  219.1 24.9 %copy-start.7 = (bf16[96,8,128]{2,1,0:T(8,128)(2,1)S(1)}, bf16[96,8,128]{2,1,0:T(8,128)(2,1)}, u32[]{:S(2)}) copy-start(bf16[96,8,128]{2,1,0:T(8,128)(2,1)} %param.19) | copy-start | bytes 589828
  (5 other events, 8.9 us)
Sparse Core Ops, SparseCore 0:
  215.6 266.4 all-reduce.4
where the time goes:
time: 493 us; the launch traced here: 492 us
  waiting for transfers between devices  258 us (52%)
  blocking collectives  100 us (20%)
  other arithmetic  43.3 us (9%)
  local copies, waits for them, and re-layouts  37.1 us (8%)
  starting transfers between devices  30.9 us (6%)
  between operations  14.9 us (3%)
  matrix products  7.92 us (2%)
    psum x1, waiting for transfers between devices, local(): lax.psum((kernel_sum, bias_sum, gain_sum, shift_sum, w_in_sum, b_in_sum,...  237 us
    psum x1, blocking collectives, local(): lax.psum((kernel_sum, bias_sum, gain_sum, shift_sum, w_in_sum, b_in_sum,...  100 us
    another operation x1, other arithmetic  23.9 us
    scatter-add x1, local copies, waits for them, and re-layouts, local(): back = back.at[:, :, breadth - 3:].add(from_right)  18.6 us
    ppermute x4, waiting for transfers between devices, from_behind(): lax.ppermute(value, axis, [(source, source + steps) for source in range(i...  12.7 us
    ppermute x2, starting transfers between devices, padded_2(): lax.ppermute(lax.slice_in_dim(block, block.shape[dim] - width, None, axis...  12.7 us
    ppermute x4, starting transfers between devices, from_behind(): lax.ppermute(value, axis, [(source, source + steps) for source in range(i...  11.4 us
  transfers between devices with their start and end apart: 9, of which 5 were waited for; matrix products, arithmetic and copies ran while one was open for 7% of the time, Pallas kernels for 0%

commit v1 on v0

--- a/solution.py
+++ b/solution.py
@@ -1,8 +1,18 @@
+import functools
 import math
 import jax
 import jax.numpy as jnp
 from jax import lax
 from jax.sharding import PartitionSpec as P
+
+
+def keep_up_circles_on(load, row_axis, which_axis):
+    for w in (row_axis, which_axis):
+        load = lax.psum(load, axis_name=w)
+    return load
+
+
+_mark_sites = functools.partial(keep_up_circles_on, row_axis="col", which_axis="row")
 
 
 def padded_2(block, sides, width):
@@ -126,9 +136,10 @@
     image_grad = (cotangent.astype(jnp.float32) + back).astype(jnp.bfloat16)
     kernel_sum = kernel_terms(conv_grad, padded)
     bias_sum = jnp.sum(conv_grad, axis=(1, 2))
-    kernel_sum, bias_sum, gain_sum, shift_sum, w_in_sum, b_in_sum, w_out_sum, scale_sum = lax.psum(
-        (kernel_sum, bias_sum, gain_sum, shift_sum, w_in_sum, b_in_sum, w_out_sum, scale_sum),
-        ("col", "row"),
+    kernel_sum, bias_sum, gain_sum, shift_sum, w_in_sum, b_in_sum, w_out_sum, scale_sum = (
+        _mark_sites(
+            (kernel_sum, bias_sum, gain_sum, shift_sum, w_in_sum, b_in_sum, w_out_sum, scale_sum)
+        )
     )
     factor = 1.0 / math.sqrt(height * lax.axis_size("row") * breadth * lax.axis_size("col"))
     return (

time: 493 us -> 1030 us (2.09)
  waiting for transfers between devices: 258 us -> 570 us
  blocking collectives: 100 us -> 304 us
  starting transfers between devices: 30.9 us -> 41.4 us
    psum x1 -> x2, waiting for transfers between devices: 237 us -> 557 us  [keep_up_circles_on(): load = lax.psum(load, axis_name=w)]
    psum x1 -> x2, blocking collectives: 100 us -> 304 us  [keep_up_circles_on(): load = lax.psum(load, axis_name=w)]
    ppermute x4, starting transfers between devices: 11.4 us -> 21.9 us  [from_behind(): lax.ppermute(value, axis, [(source, source + steps) for source in range(i...]
  transfers between devices with their start and end apart: 9 -> 10, of which waited for: 5 -> 5; matrix products, arithmetic and copies ran while one was open for 7% -> 4% of each run, Pallas kernels for 0% -> 0%
where the time goes in v1:
time: 1030 us; the launch traced here: 1020 us
  waiting for transfers between devices  570 us (55%)
  blocking collectives  304 us (30%)
  other arithmetic  45.6 us (4%)
  starting transfers between devices  41.4 us (4%)
  local copies, waits for them, and re-layouts  39.9 us (4%)
  between operations  15.6 us (2%)
    psum x2, waiting for transfers between devices, keep_up_circles_on(): load = lax.psum(load, axis_name=w)  557 us
    psum x2, blocking collectives, keep_up_circles_on(): load = lax.psum(load, axis_name=w)  304 us
    another operation x1, other arithmetic  24.1 us
    ppermute x4, starting transfers between devices, from_behind(): lax.ppermute(value, axis, [(source, source + steps) for source in range(i...  21.9 us
  transfers between devices with their start and end apart: 10, of which 5 were waited for; matrix products, arithmetic and copies ran while one was open for 4% of the time, Pallas kernels for 0%

profile of v1, /device:TPU:1, one launch (start us, length us, event | category | flops | bytes accessed | tf_op | source)
XLA Modules:
  0.0 1024.6 jit_solution(15034810615370859510)
XLA Ops:
  7.2 1.1 copy.20
  8.4 4.6 collective-permute-start
  13.0 5.5 collective-permute-start.1
  18.5 1.0 slice_bitcast_fusion.48
  19.5 1.0 slice_bitcast_fusion.47
  20.7 8.0 collective-permute-start.2
  28.7 1.3 collective-permute-start.3
  30.0 0.9 slice_bitcast_fusion.46
  31.0 1.0 convert.8
  32.0 0.9 copy.77
  32.9 7.4 collective-permute-done.3
  40.5 4.3 fusion.223
  45.6 1.7 fusion.107
  47.4 2.0 convert_reduce_fusion
  49.3 1.0 fusion.220
  50.7 0.8 fusion.207
  51.9 1.9 fusion.203
  53.9 1.9 fusion.153
  55.8 0.8 fusion.135
  56.9 24.1 %fusion.221 = (bf16[96,14,134]{2,1,0:T(8,128)(2,1)}, f32[96,14,134]{2,1,0:T(8,128)S(1)}) fusion(f32[96]{0:T(128)S(1)} %get-tuple-element.154, f32[96]{0:T(128)S(1)} %get-tuple-element.173, f32[96]{0:T(128)S(1)} %copy-done.31, f32[96]{0:T(128)S(1)} %copy-done.47, f32[96]{0:T(128)S(1)} %copy-done.45, f32[96]{0:T(128)S(1)} %copy-done.43, f32[96]{0:T(128)S(1)} %copy-done.41, ...), kind=kLoop, calls=%fused_computation.460 | loop fusion | flops 17649408 | bytes 1492608 | tf_op jit(solution)/shard_map/convert.3
  81.2 1.0 fusion.215
  82.2 1.6 fusion.185
  84.1 2.9 stack.199
  87.1 1.8 fusion.206
  89.0 260.9 %all-reduce.1 = (f32[96,7,7]{0,2,1:T(8,128)S(1)}, f32[96]{0:T(128)S(1)}, f32[96]{0:T(128)S(1)}, f32[96]{0:T(128)S(1)}, f32[384]{0:T(512)S(1)}, /*index=5*/f32[96]{0:T(128)S(1)}) all-reduce(f32[96,7,7]{0,2,1:T(8,128)S(1)} %reshape.203, f32[96]{0:T(128)S(1)} %copy-done.55, ...), channel_id=1, replica_groups=mesh['col'=64,'row'=8] {'col'}, use_global_device_ids=true, to_apply=%region_53.54 | all-reduce | flops 5472 | bytes 43776 | tf_op jit(solution)/shard_map/psum | solution.py:11
  349.9 42.8 %all-reduce.3 = (f32[96,7,7]{0,2,1:T(8,128)S(1)}, f32[96]{0:T(128)S(1)}, f32[96]{0:T(128)S(1)}, f32[96]{0:T(128)S(1)}, f32[384]{0:T(512)S(1)}, /*index=5*/f32[96]{0:T(128)S(1)}) all-reduce(f32[96,7,7]{0,2,1:T(8,128)S(1)} %get-tuple-element.121, f32[96]{0:T(128)S(1)} %get-tuple-element.122, ...), channel_id=1, replica_groups=mesh['col'=64,'row'=8] {'row'}, use_global_device_ids=true, to_apply=%region_54.55 | all-reduce | flops 5472 | bytes 43776 | tf_op jit(solution)/shard_map/psum | solution.py:11
  392.7 0.6 broadcast_multiply_fusion.2
  393.3 0.6 broadcast_multiply_fusion.6
  394.4 0.5 broadcast_multiply_fusion.7
  395.1 3.9 collective-permute-start.4
  399.0 0.5 broadcast_multiply_fusion.8
  399.6 1.3 collective-permute-start.5
  401.0 0.6 collective-permute-done.4
  401.8 2.6 scatter-add.14
  404.4 5.7 collective-permute-done.5
  410.1 1.1 slice_add_fusion.2
  411.1 2.6 scatter-add.15
  413.9 10.5 %collective-permute-start.6 = (f32[96,8,3]{2,1,0:T(8,128)S(1)}, f32[96,8,3]{2,1,0:T(8,128)S(1)}, u32[]{:S(2)}, u32[]{:S(2)}) collective-permute-start(f32[96,8,3]{2,1,0:T(8,128)S(1)} %get-tuple-element.143), channel_id=1, source_target_pairs={{0,8},{8,16},{16,24},{24,32},{32,40},{40,48},{48,56},{56,64},{64,7... | collective-permute-start | bytes 27656 | tf_op jit(solution)/shard_map/ppermute | solution.py:34
  424.4 0.5 broadcast_multiply_fusion.9
  425.0 0.7 copy.79
  425.8 6.2 collective-permute-start.7
  432.2 6.1 scatter-add.16
  438.3 467.0 %all-reduce.8.cloned.1.call-done = (f32[96,384]{1,0:T(8,128)}, f32[384,96]{0,1:T(8,128)}) async-done(((f32[96,384]{1,0:T(8,128)}, f32[384,96]{0,1:T(8,128)}), (f32[96,384]{1,0:T(8,128)}, f32[384,96]{0,1:T(8,128)})) %all-reduce.8.cloned.1.call-update) | async-done | bytes 294928 | tf_op jit(solution)/shard_map/psum | solution.py:11
  905.5 18.6 %scatter-add.19 = f32[96,8,128]{2,1,0:T(8,128)S(1)} dynamic-update-slice(f32[96,8,128]{2,1,0:T(8,128)S(1)} %scatter-add.16, f32[96,8,3]{2,1,0:T(8,128)S(1)} %slice_add_fusion, s32[]{:T(128)} %constant.134.clone.1, s32[]{:T(128)} %constant.134.clone.1, s32[]{:T(128)} %constant.136.clone.1) | dynamic-update-slice | bytes 18436 | tf_op jit(solution)/shard_map/scatter-add | solution.py:135
  924.1 0.7 add_convert_fusion
  924.8 89.8 %all-reduce.10.cloned.1.call-done = (f32[96,384]{1,0:T(8,128)}, f32[384,96]{0,1:T(8,128)}) async-done(((f32[96,384]{1,0:T(8,128)}, f32[384,96]{0,1:T(8,128)}), (f32[96,384]{1,0:T(8,128)}, f32[384,96]{0,1:T(8,128)})) %all-reduce.10.cloned.1.call-update) | async-done | bytes 294928 | tf_op jit(solution)/shard_map/psum | solution.py:11
  1014.6 1.6 broadcast_multiply_fusion
  1016.1 1.6 broadcast_multiply_fusion.1
  (204 shorter events, 3.7 us)
Async XLA Ops:
  7.2 38.4 %copy-start = (bf16[96,384]{1,0:T(8,128)(2,1)S(1)}, bf16[96,384]{1,0:T(8,128)(2,1)}, u32[]{:S(2)}) copy-start(bf16[96,384]{1,0:T(8,128)(2,1)} %param.24) | copy-start | bytes 221188
  7.2 898.1 %all-reduce.8.cloned.1.call-start = ((), (), s32[]{:S(2)}) async-start(), calls=%async_computation | async-start | bytes 589824 | tf_op jit(solution)/shard_map/psum | solution.py:11
  8.4 32.1 %copy-start.84 = (f32[96]{0:T(128)S(1)}, f32[96]{0:T(128)}, u32[]{:S(2)}) copy-start(f32[96]{0:T(128)} %param.21) | copy-start | bytes 1156
  8.4 12.2 %collective-permute-start = (bf16[96,8,3]{0,2,1:T(4,128)(2,1)S(1)}, bf16[96,8,3]{0,2,1:T(4,128)(2,1)S(1)}, u32[]{:S(2)}, u32[]{:S(2)}) collective-permute-start(bf16[96,8,3]{0,2,1:T(4,128)(2,1)S(1)} %get-tuple-element.152), channel_id=1, source_target_pairs={{0,8},{8,16},{16,24},{24,32},{32,40},{40,48},{48,56},{56,64},{64,7... | collective-permute-start | bytes 13832 | tf_op jit(solution)/shard_map/ppermute | solution.py:23
  13.0 7.6 collective-permute-start.1
  20.5 24.3 %copy-start.10 = (f32[96]{0:T(128)}, f32[96]{0:T(128)S(1)}, u32[]{:S(2)}) copy-start(f32[96]{0:T(128)S(1)} %get-tuple-element.182) | copy-start | bytes 1156
  20.5 24.3 %copy-start.12 = (f32[96]{0:T(128)}, f32[96]{0:T(128)S(1)}, u32[]{:S(2)}) copy-start(f32[96]{0:T(128)S(1)} %get-tuple-element.183) | copy-start | bytes 1156
  20.5 24.3 %copy-start.14 = (f32[96]{0:T(128)}, f32[96]{0:T(128)S(1)}, u32[]{:S(2)}) copy-start(f32[96]{0:T(128)S(1)} %get-tuple-element.184) | copy-start | bytes 1156
  20.5 24.3 %copy-start.16 = (f32[96]{0:T(128)}, f32[96]{0:T(128)S(1)}, u32[]{:S(2)}) copy-start(f32[96]{0:T(128)S(1)} %get-tuple-element.185) | copy-start | bytes 1156
  20.5 24.3 %copy-start.18 = (f32[96]{0:T(128)}, f32[96]{0:T(128)S(1)}, u32[]{:S(2)}) copy-start(f32[96]{0:T(128)S(1)} %get-tuple-element.186) | copy-start | bytes 1156
  20.5 24.3 %copy-start.20 = (f32[96]{0:T(128)}, f32[96]{0:T(128)S(1)}, u32[]{:S(2)}) copy-start(f32[96]{0:T(128)S(1)} %get-tuple-element.187) | copy-start | bytes 1156
  20.5 24.3 %copy-start.22 = (f32[96]{0:T(128)}, f32[96]{0:T(128)S(1)}, u32[]{:S(2)}) copy-start(f32[96]{0:T(128)S(1)} %get-tuple-element.188) | copy-start | bytes 1156
  20.5 24.3 %copy-start.24 = (f32[96]{0:T(128)}, f32[96]{0:T(128)S(1)}, u32[]{:S(2)}) copy-start(f32[96]{0:T(128)S(1)} %get-tuple-element.189) | copy-start | bytes 1156
  20.6 24.3 %copy-start.26 = (f32[96]{0:T(128)}, f32[96]{0:T(128)S(1)}, u32[]{:S(2)}) copy-start(f32[96]{0:T(128)S(1)} %get-tuple-element.190) | copy-start | bytes 1156
  20.6 24.3 %copy-start.28 = (f32[96]{0:T(128)}, f32[96]{0:T(128)S(1)}, u32[]{:S(2)}) copy-start(f32[96]{0:T(128)S(1)} %get-tuple-element.191) | copy-start | bytes 1156
  20.7 12.2 %collective-permute-start.2 = (bf16[96,3,134]{0,2,1:T(8,128)(2,1)S(1)}, bf16[96,3,134]{0,2,1:T(8,128)(2,1)S(1)}, u32[]{:S(2)}, u32[]{:S(2)}) collective-permute-start(bf16[96,3,134]{0,2,1:T(8,128)(2,1)S(1)} %get-tuple-element.150), channel_id=1, source_target_pairs={{0,1},{1,2},{2,3},{3,4},{4,5},{5,6},{6,7},{8,9},{9,10},{10,11},{11... | collective-permute-start | bytes 231560 | tf_op jit(solution)/shard_map/ppermute | solution.py:23
  28.7 11.6 %collective-permute-start.3 = (bf16[96,3,134]{0,2,1:T(8,128)(2,1)S(1)}, bf16[96,3,134]{0,2,1:T(8,128)(2,1)S(1)}, u32[]{:S(2)}, u32[]{:S(2)}) collective-permute-start(bf16[96,3,134]{0,2,1:T(8,128)(2,1)S(1)} %get-tuple-element.151), channel_id=1, source_target_pairs={{1,0},{2,1},{3,2},{4,3},{5,4},{6,5},{7,6},{9,8},{10,9},{11,10},{12... | collective-permute-start | bytes 231560 | tf_op jit(solution)/shard_map/ppermute | solution.py:26
  30.9 14.0 %copy-start.30 = (f32[96]{0:T(128)}, f32[96]{0:T(128)S(1)}, u32[]{:S(2)}) copy-start(f32[96]{0:T(128)S(1)} %get-tuple-element.192) | copy-start | bytes 1156
  30.9 14.0 %copy-start.32 = (f32[96]{0:T(128)}, f32[96]{0:T(128)S(1)}, u32[]{:S(2)}) copy-start(f32[96]{0:T(128)S(1)} %get-tuple-element.193) | copy-start | bytes 1156
  30.9 14.0 %copy-start.34 = (f32[96]{0:T(128)}, f32[96]{0:T(128)S(1)}, u32[]{:S(2)}) copy-start(f32[96]{0:T(128)S(1)} %get-tuple-element.194) | copy-start | bytes 1156
  30.9 14.0 %copy-start.36 = (f32[96]{0:T(128)}, f32[96]{0:T(128)S(1)}, u32[]{:S(2)}) copy-start(f32[96]{0:T(128)S(1)} %get-tuple-element.195) | copy-start | bytes 1156
  30.9 14.0 %copy-start.38 = (f32[96]{0:T(128)}, f32[96]{0:T(128)S(1)}, u32[]{:S(2)}) copy-start(f32[96]{0:T(128)S(1)} %get-tuple-element.196) | copy-start | bytes 1156
  30.9 14.0 %copy-start.40 = (f32[96]{0:T(128)}, f32[96]{0:T(128)S(1)}, u32[]{:S(2)}) copy-start(f32[96]{0:T(128)S(1)} %get-tuple-element.197) | copy-start | bytes 1156
  31.0 14.0 %copy-start.42 = (f32[96]{0:T(128)}, f32[96]{0:T(128)S(1)}, u32[]{:S(2)}) copy-start(f32[96]{0:T(128)S(1)} %get-tuple-element.198) | copy-start | bytes 1156
  31.0 14.0 %copy-start.44 = (f32[96]{0:T(128)}, f32[96]{0:T(128)S(1)}, u32[]{:S(2)}) copy-start(f32[96]{0:T(128)S(1)} %get-tuple-element.199) | copy-start | bytes 1156
  31.0 14.0 %copy-start.46 = (f32[96]{0:T(128)}, f32[96]{0:T(128)S(1)}, u32[]{:S(2)}) copy-start(f32[96]{0:T(128)S(1)} %get-tuple-element.200) | copy-start | bytes 1156
  31.0 14.0 %copy-start.48 = (f32[96]{0:T(128)}, f32[96]{0:T(128)S(1)}, u32[]{:S(2)}) copy-start(f32[96]{0:T(128)S(1)} %get-tuple-element.201) | copy-start | bytes 1156
  31.0 14.0 %copy-start.50 = (f32[96]{0:T(128)}, f32[96]{0:T(128)S(1)}, u32[]{:S(2)}) copy-start(f32[96]{0:T(128)S(1)} %get-tuple-element.202) | copy-start | bytes 1156
  32.0 15.4 %copy-start.3 = (f32[12,8,8,128]{3,2,1,0:T(8,128)}, f32[12,8,8,128]{3,2,1,0:T(8,128)S(1)}, u32[]{:S(2)}) copy-start(f32[12,8,8,128]{3,2,1,0:T(8,128)S(1)} %convert.8) | copy-start | bytes 1179652
  40.4 5.1 copy-start.9
  40.5 5.1 copy-start.85
  40.5 5.1 copy-start.86
  53.7 2.9 copy-start.11
  53.7 2.9 copy-start.13
  53.7 2.9 copy-start.15
  56.8 24.2 %copy-start.4 = (f32[12,8,8,128]{3,2,1,0:T(8,128)S(1)}, f32[12,8,8,128]{3,2,1,0:T(8,128)}, u32[]{:S(2)}) copy-start(f32[12,8,8,128]{3,2,1,0:T(8,128)} %copy-done.3) | copy-start | bytes 1179652
  56.9 24.2 %copy-start.5 = (bf16[384,1024]{0,1:T(8,128)(2,1)S(1)}, bf16[384,1024]{0,1:T(8,128)(2,1)}, u32[]{:S(2)}) copy-start(bf16[384,1024]{0,1:T(8,128)(2,1)} %get-tuple-element.205) | copy-start | bytes 2359300
  81.2 5.9 copy-start.53
  83.8 5.2 copy-start.54
  83.8 5.2 copy-start.55
  83.8 5.2 copy-start.83
  83.8 311.2 %copy-start.6 = (bf16[96,14,134]{2,1,0:T(8,128)(2,1)S(1)}, bf16[96,14,134]{2,1,0:T(8,128)(2,1)}, u32[]{:S(2)}) copy-start(bf16[96,14,134]{2,1,0:T(8,128)(2,1)} %get-tuple-element.137) | copy-start | bytes 1080580
  395.1 6.5 collective-permute-start.4
  399.6 10.4 %collective-permute-start.5 = (bf16[96,3,134]{2,1,0:T(4,128)(2,1)S(1)}, bf16[96,3,134]{2,1,0:T(4,128)(2,1)}, u32[]{:S(2)}, u32[]{:S(2)}) collective-permute-start(bf16[96,3,134]{2,1,0:T(4,128)(2,1)S(1)} %get-tuple-element.144), channel_id=1, source_target_pairs={{1,0},{2,1},{3,2},{4,3},{5,4},{6,5},{7,6},{9,8},{10,9},{11,10},{12... | collective-permute-start | bytes 231560 | tf_op jit(solution)/shard_map/ppermute | solution.py:34
  401.0 613.6 %all-reduce.10.cloned.1.call-start = ((), (), s32[]{:S(2)}) async-start(), calls=%async_computation.1 | async-start | bytes 589824 | tf_op jit(solution)/shard_map/psum | solution.py:11
  413.9 18.1 %collective-permute-start.6 = (f32[96,8,3]{2,1,0:T(8,128)S(1)}, f32[96,8,3]{2,1,0:T(8,128)S(1)}, u32[]{:S(2)}, u32[]{:S(2)}) collective-permute-start(f32[96,8,3]{2,1,0:T(8,128)S(1)} %get-tuple-element.143), channel_id=1, source_target_pairs={{0,8},{8,16},{16,24},{24,32},{32,40},{40,48},{48,56},{56,64},{64,7... | collective-permute-start | bytes 27656 | tf_op jit(solution)/shard_map/ppermute | solution.py:34
  425.8 479.5 %collective-permute-start.7 = (f32[96,8,3]{2,1,0:T(8,128)S(1)}, f32[96,8,3]{2,1,0:T(8,128)S(1)}, u32[]{:S(2)}, u32[]{:S(2)}) collective-permute-start(f32[96,8,3]{2,1,0:T(8,128)S(1)} %get-tuple-element.142), channel_id=1, source_target_pairs={{8,0},{16,8},{24,16},{32,24},{40,32},{48,40},{56,48},{64,56},{72,6... | collective-permute-start | bytes 27656 | tf_op jit(solution)/shard_map/ppermute | solution.py:34
  432.2 491.9 %copy-start.7 = (bf16[96,8,128]{2,1,0:T(8,128)(2,1)S(1)}, bf16[96,8,128]{2,1,0:T(8,128)(2,1)}, u32[]{:S(2)}) copy-start(bf16[96,8,128]{2,1,0:T(8,128)(2,1)} %param.19) | copy-start | bytes 589828
  (49 other events, 136.4 us)
Sparse Core Ops, SparseCore 0:
  401.1 504.1 all-reduce.7
  908.6 105.9 all-reduce.9
